TPU v7x, 32 devices: a whole 2x2x4 slice. The times are simulated.
32 devices in a mesh: sta: 4 (over y, x), evt: 8 (over z, core).
Axes of the slice: x: 2, y: 2, z: 4, core: 2. Of those that a mesh axis runs over, the one named last changes fastest.
Arguments:
- traces: bfloat16 [512, 96, 280], P('evt', 'sta'), may hold values from -400 to 400, as said below
- channel_valid: int32 [96], P('sta'), may hold values 0 or 1
- partner_block: int32 [512, 2], P('evt'), may hold values from 0 to 7, all different within a row; in each aligned block of 64 rows (0 to 63, 64 to 127, ...) at most 16 rows name the same one
Outputs:
- coefficient: float32 [512, 81, 128], P('evt')
Inputs may be any that keep to these rules, and one draw needn't show every extreme that they name: `partner_block`: each event names 2 different blocks; among the 64 events of one block no block is named more than 16 times, and some block is named exactly 16 times. `traces`: finite trace samples.
All inputs are finite; a program needn't handle non-finite values. No bound on the sum of `channel_valid` on one device may be relied on, other than what follows from the above.
Results may differ from a plain program's by a relative error of at most 0.0003.
Values may be sent and summed in bfloat16 or wider, within the bound.
No kernel may reach another device: no remote copies, remote signals or barrier semaphores. Data moves between devices by JAX's collectives and lax.ppermute only.
A program may use at most 64 MiB of HBM per device.

v0:
```python
import jax
import jax.numpy as jnp
from jax import lax
from jax.sharding import PartitionSpec as P

WIN = 200
MAXLAG = 40


def band_table(extent, lag_count):
    sample = jnp.arange(extent, dtype=jnp.int32)[:, None]
    shift = jnp.arange(lag_count, dtype=jnp.int32)[None, :]
    return ((sample >= shift) & (sample < shift + WIN)).astype(jnp.float32)


def normalize(lag_scores, slot_energy, event_energy):
    return lag_scores / jnp.sqrt(event_energy[:, None, None] * slot_energy[None, :, :] + 1e-06)


def body(traces, channel_valid, partner_block):
    events, channels, extent = traces.shape
    partners = partner_block.shape[1]
    devices_evt = lax.axis_size("evt")
    capacity = max(2, (events * partners + devices_evt - 1) // devices_evt)
    slot_count = devices_evt * capacity
    lag_count = extent - WIN + 1
    flat = partner_block.reshape(-1)
    owner_hot = (flat[:, None] == jnp.arange(devices_evt, dtype=jnp.int32)[None, :]).astype(
        jnp.int32
    )
    before = jnp.cumsum(owner_hot, axis=0) - owner_hot
    ranking = jnp.sum(before * owner_hot, axis=1)
    target = flat * capacity + ranking
    slot_hot = (target[:, None] == jnp.arange(slot_count, dtype=jnp.int32)[None, :]).astype(
        jnp.bfloat16
    )
    row_event = jnp.arange(events * partners, dtype=jnp.int32) // partners
    event_hot = (row_event[:, None] == jnp.arange(events, dtype=jnp.int32)[None, :]).astype(
        jnp.bfloat16
    )
    selection = jnp.dot(slot_hot.T, event_hot, preferred_element_type=jnp.float32).astype(
        jnp.bfloat16
    )
    outgoing = jnp.dot(
        selection, traces.reshape(events, channels * extent), preferred_element_type=jnp.float32
    ).astype(jnp.bfloat16)
    received = lax.all_to_all(
        outgoing.reshape(slot_count, channels, extent),
        "evt",
        split_axis=0,
        concat_axis=0,
        tiled=True,
    )
    valid = channel_valid.astype(jnp.bfloat16)
    template = traces[:, :, MAXLAG : MAXLAG + WIN] * valid[None, :, None]
    lag_scores = lax.conv_general_dilated(
        received,
        template,
        (1,),
        "VALID",
        dimension_numbers=("NCH", "OIH", "CHN"),
        preferred_element_type=jnp.float32,
    )
    event_energy = jnp.sum(jnp.square(template.astype(jnp.float32)), axis=(1, 2))
    squares_sum = jnp.sum(
        jnp.square(received.astype(jnp.float32)) * channel_valid.astype(jnp.float32)[None, :, None],
        axis=1,
    )
    slot_energy = lax.dot_general(
        band_table(extent, lag_count),
        squares_sum,
        (((0,), (1,)), ((), ())),
        precision=lax.Precision.HIGHEST,
    )
    scores_all, slot_all, event_all = lax.psum((lag_scores, slot_energy, event_energy), "sta")
    return normalize(scores_all, slot_all, event_all)


def solution(mesh):
    return jax.shard_map(
        body,
        mesh=mesh,
        in_specs=(P("evt", "sta", None), P("sta"), P("evt", None)),
        out_specs=P("evt", None, None),
        check_vma=False,
    )
```

profile of v0, /device:TPU:0, one launch (start us, length us, event | category | flops | bytes accessed | tf_op | source)
XLA Modules:
  0.0 186.9 jit_solution(16003686548078030480)
XLA Ops:
  6.5 0.8 copy.20
  7.3 0.1 reshape.40
  7.4 0.1 fusion.4
  7.5 0.2 reduce_window_sum.11
  7.7 0.2 select_reduce_fusion
  7.9 2.1 %reshape.41 = bf16[64,6720]{1,0:T(8,128)(2,1)S(1)} reshape(bf16[64,24,280]{2,1,0:T(8,128)(2,1)} %param.3) | data formatting | bytes 1720320 | tf_op jit(solution)/shard_map/reshape | solution.py:45
  10.0 0.9 convolution_convert_fusion
  11.0 2.7 %copy.21 = bf16[128,24,280]{2,1,0:T(8,128)(2,1)} copy(bf16[128,24,280]{0,2,1:T(8,128)(2,1)S(1)} %bitcast.5) | data formatting | bytes 3440640 | tf_op jit(solution)/shard_map/reshape | solution.py:48
  13.7 0.0 copy-start.1
  13.7 0.0 copy-start
  13.7 6.5 %all-to-all-start = ((bf16[128,24,280]{2,1,0:T(8,128)(2,1)}), bf16[128,24,280]{2,1,0:T(8,128)(2,1)S(1)}, u32[]{:S(2)}, u32[]{:S(2)}) async-start(bf16[128,24,280]{2,1,0:T(8,128)(2,1)} %copy.21), calls=%async_computation | async-start | bytes 4718592 | tf_op jit(solution)/shard_map/all_to_all | solution.py:47
  20.2 0.0 all-reduce.3.cloned.1.call-start
  20.2 0.0 copy-done.1
  20.2 0.0 copy-done
  20.2 1.8 multiply_reduce_fusion.1
  22.0 2.9 %copy.23 = bf16[64,24,200]{0,1,2:T(8,128)(2,1)} copy(bf16[64,24,200]{2,1,0:T(8,128)(2,1)} %get-tuple-element.8) | data formatting | bytes 1228800 | tf_op jit(solution)/shard_map/mul | solution.py:55
  24.9 50.0 %all-to-all-done = bf16[128,24,280]{2,1,0:T(8,128)(2,1)S(1)} async-done(((bf16[128,24,280]{2,1,0:T(8,128)(2,1)}), bf16[128,24,280]{2,1,0:T(8,128)(2,1)S(1)}, u32[]{:S(2)}, u32[]{:S(2)}) %all-to-all-start) | async-done | bytes 1720352 | tf_op jit(solution)/shard_map/all_to_all | solution.py:47
  74.8 3.0 %copy.22 = bf16[128,24,280]{0,1,2:T(8,128)(2,1)} copy(bf16[128,24,280]{2,1,0:T(8,128)(2,1)S(1)} %all-to-all-done) | data formatting | bytes 3440640 | tf_op jit(solution)/shard_map/all_to_all | solution.py:47
  77.8 18.6 %fusion.10 = f32[64,81,128]{2,0,1:T(8,128)} fusion(bf16[128,24,280]{0,1,2:T(8,128)(2,1)} %copy.22, bf16[64,24,200]{0,1,2:T(8,128)(2,1)} %copy.23), kind=kOutput, calls=%fused_computation.25 | convolution fusion | flops 6370099200 | bytes 4988928 | tf_op jit(solution)/shard_map/conv_general_dilated | solution.py:56
  96.5 0.0 all-reduce.3.cloned.1.call-update
  96.5 2.6 %copy.24 = bf16[128,24,280]{0,2,1:T(8,128)(2,1)} copy(bf16[128,24,280]{2,1,0:T(8,128)(2,1)S(1)} %all-to-all-done) | data formatting | bytes 3440640 | tf_op jit(solution)/shard_map/all_to_all | solution.py:47
  99.1 1.9 %multiply_reduce_fusion = f32[128,280]{0,1:T(8,128)S(1)} fusion(bf16[128,24,280]{0,2,1:T(8,128)(2,1)} %copy.24, f32[24]{0:T(128)S(1)} %get-tuple-element.9), kind=kLoop, calls=%fused_computation.1 | loop fusion | flops 3404800 | bytes 1863776 | tf_op jit(solution)/shard_map/reduce_sum | solution.py:65
  101.0 0.3 fusion.1
  101.4 18.1 %all-reduce = (f32[81,128]{1,0:T(8,128)S(1)}, f32[64]{0:T(128)S(1)}) all-reduce(f32[81,128]{1,0:T(8,128)S(1)} %fusion.1, f32[64]{0:T(128)S(1)} %get-tuple-element.7), channel_id=1, replica_groups=mesh['sta'=4,'evt'=8] {'sta'}, use_global_device_ids=true, to_apply=%region_6.7 | all-reduce | flops 10432 | bytes 83456 | tf_op jit(solution)/shard_map/psum | solution.py:75
  119.5 56.7 %all-reduce.3.cloned.1.call-done = f32[64,81,128]{2,0,1:T(8,128)} async-done(((f32[64,81,128]{2,0,1:T(8,128)}), f32[64,81,128]{2,0,1:T(8,128)}) %all-reduce.3.cloned.1.call-update) | async-done | bytes 2654224 | tf_op jit(solution)/shard_map/psum | solution.py:75
  176.1 4.0 %rsqrt_multiply_fusion = f32[64,81,128]{2,0,1:T(8,128)} fusion(f32[64,81,128]{2,0,1:T(8,128)} %all-reduce.3.cloned.1.call-done, f32[81,128]{1,0:T(8,128)S(1)} %get-tuple-element.5, f32[64]{0:T(128)S(1)} %get-tuple-element.6), kind=kLoop, calls=%fused_computation.2 | loop fusion | flops 1990656 | bytes 5350144 | tf_op jit(solution)/shard_map/div | solution.py:17
  (3 shorter events, 0.0 us)
Async XLA Ops:
  13.7 6.5 %copy-start.1 = (s32[24]{0:T(128)S(1)}, s32[24]{0:T(128)}, u32[]{:S(2)}) copy-start(s32[24]{0:T(128)} %param.4) | copy-start | bytes 292
  13.7 6.5 %copy-start = (bf16[64,24,280]{2,1,0:T(8,128)(2,1)S(1)}, bf16[64,24,280]{2,1,0:T(8,128)(2,1)}, u32[]{:S(2)}) copy-start(bf16[64,24,280]{2,1,0:T(8,128)(2,1)} %param.3) | copy-start | bytes 2580484
  13.7 61.1 %all-to-all-start = ((bf16[128,24,280]{2,1,0:T(8,128)(2,1)}), bf16[128,24,280]{2,1,0:T(8,128)(2,1)S(1)}, u32[]{:S(2)}, u32[]{:S(2)}) async-start(bf16[128,24,280]{2,1,0:T(8,128)(2,1)} %copy.21), calls=%async_computation | async-start | bytes 4718592 | tf_op jit(solution)/shard_map/all_to_all | solution.py:47
  20.2 156.0 %all-reduce.3.cloned.1.call-start = ((), (), s32[]{:S(2)}) async-start(), calls=%async_computation.1 | async-start | bytes 5308416 | tf_op jit(solution)/shard_map/psum | solution.py:75
Sparse Core Ops, SparseCore 0:
  96.6 79.4 all-reduce.2
where the time goes:
time: 187 us
  waiting for transfers between devices  107 us (57%)
  matrix products  19.9 us (11%)
  blocking collectives  18.1 us (10%)
  local copies, waits for them, and re-layouts  14.2 us (8%)
  between operations  13.5 us (7%)
  other arithmetic  8.11 us (4%)
  starting transfers between devices  6.49 us (3%)
    psum x1, waiting for transfers between devices, body(): lax.psum((lag_scores, slot_energy, event_energy), 'sta')  56.7 us
    all_to_all x1, waiting for transfers between devices, body(): lax.all_to_all(outgoing.reshape(slot_count, channels, extent), 'evt', spl...  50 us
    conv_general_dilated x1, matrix products, body(): lax.conv_general_dilated(received, template, (1,), 'VALID', dimension_num...  18.6 us
    psum x1, blocking collectives, body(): lax.psum((lag_scores, slot_energy, event_energy), 'sta')  18.1 us
    all_to_all x1, starting transfers between devices, body(): lax.all_to_all(outgoing.reshape(slot_count, channels, extent), 'evt', spl...  6.46 us
    all_to_all x2, local copies, waits for them, and re-layouts, body(): lax.all_to_all(outgoing.reshape(slot_count, channels, extent), 'evt', spl...  5.57 us
    div x1, other arithmetic, normalize(): lag_scores / jnp.sqrt(event_energy[:, None, None] * slot_energy[None, :,...  3.95 us
  transfers between devices with their start and end apart: 2, of which 2 were waited for; matrix products, arithmetic and copies ran while one was open for 5% of the time, Pallas kernels for 0%

commit v1 on v0

v1 whole, which is shorter than its diff:
```python
import jax
import jax.numpy as jnp
from jax import lax
from jax.sharding import PartitionSpec as P

WIN = 200
MAXLAG = 40


def band_table(extent, lag_count):
    sample = jnp.arange(extent, dtype=jnp.int32)[:, None]
    shift = jnp.arange(lag_count, dtype=jnp.int32)[None, :]
    return ((sample >= shift) & (sample < shift + WIN)).astype(jnp.float32)


def body(traces, channel_valid, partner_block):
    events, channels, extent = traces.shape
    partners = partner_block.shape[1]
    devices_evt = lax.axis_size("evt")
    capacity = max(2, (events * partners + devices_evt - 1) // devices_evt)
    slot_count = devices_evt * capacity
    lag_count = extent - WIN + 1
    chunks = 4 if capacity % 4 == 0 else (2 if capacity % 2 == 0 else 1)
    per = capacity // chunks
    flat = partner_block.reshape(-1)
    owner_hot = (flat[:, None] == jnp.arange(devices_evt, dtype=jnp.int32)[None, :]).astype(
        jnp.int32
    )
    before = jnp.cumsum(owner_hot, axis=0) - owner_hot
    ranking = jnp.sum(before * owner_hot, axis=1)
    target = flat * capacity + ranking
    slot_hot = (target[:, None] == jnp.arange(slot_count, dtype=jnp.int32)[None, :]).astype(
        jnp.bfloat16
    )
    row_event = jnp.arange(events * partners, dtype=jnp.int32) // partners
    event_hot = (row_event[:, None] == jnp.arange(events, dtype=jnp.int32)[None, :]).astype(
        jnp.bfloat16
    )
    selection = jnp.dot(slot_hot.T, event_hot, preferred_element_type=jnp.float32).astype(
        jnp.bfloat16
    )
    outgoing = jnp.dot(
        selection, traces.reshape(events, channels * extent), preferred_element_type=jnp.float32
    ).astype(jnp.bfloat16)
    outgoing = outgoing.reshape(devices_evt, chunks, per, channels, extent)
    valid = channel_valid.astype(jnp.bfloat16)
    valid_wide = channel_valid.astype(jnp.float32)
    template = traces[:, :, MAXLAG : MAXLAG + WIN] * valid[None, :, None]
    event_energy = jnp.sum(jnp.square(template.astype(jnp.float32)), axis=(1, 2))
    band = band_table(extent, lag_count)
    width = devices_evt * per
    parts = []
    energies = []
    pending = None
    previous = None

    def reduce_pending(pending, previous):
        if previous is not None:
            previous, pending = lax.optimization_barrier((previous, pending))
            parts[-1] = (previous[:events], previous[events])
        total = lax.psum(pending, "sta")
        if not parts:
            energies.append(total[events + 1].reshape(-1)[:events])
        parts.append((total[:events], total[events]))
        return total

    for c in range(chunks):
        sending = outgoing[:, c].reshape(width, channels, extent)
        if pending is not None:
            pending, sending = lax.optimization_barrier((pending, sending))
        received = lax.all_to_all(sending, "evt", split_axis=0, concat_axis=0, tiled=True)
        if pending is not None:
            previous = reduce_pending(pending, previous)
        lag_scores = lax.conv_general_dilated(
            received,
            template,
            (1,),
            "VALID",
            dimension_numbers=("NCH", "OIH", "CHN"),
            preferred_element_type=jnp.float32,
        )
        squares_sum = jnp.sum(
            jnp.square(received.astype(jnp.float32)) * valid_wide[None, :, None], axis=1
        )
        slot_energy = lax.dot_general(
            band, squares_sum, (((0,), (1,)), ((), ())), precision=lax.Precision.HIGHEST
        )
        rows = [lag_scores, slot_energy[None]]
        if c == 0:
            pad = jnp.zeros((lag_count * width - events,), jnp.float32)
            rows.append(jnp.concatenate([event_energy, pad]).reshape(1, lag_count, width))
        pending = jnp.concatenate(rows, axis=0)
    previous = reduce_pending(pending, previous)
    energy_all = energies[0]
    outs = []
    for scores_all, slot_all in parts:
        outs.append(
            scores_all
            / jnp.sqrt(energy_all[:, None, None] * slot_all[None, :, :] + 1e-06)
        )
    coef = jnp.stack(outs, axis=0).reshape(chunks, events, lag_count, devices_evt, per)
    return jnp.transpose(coef, (1, 2, 3, 0, 4)).reshape(events, lag_count, slot_count)


def solution(mesh):
    return jax.shard_map(
        body,
        mesh=mesh,
        in_specs=(P("evt", "sta", None), P("sta"), P("evt", None)),
        out_specs=P("evt", None, None),
        check_vma=False,
    )
```

time: 187 us -> 418 us (2.24); the launches traced: 187 us -> 411 us
  matrix products: 19.9 us -> 111 us
  waiting for transfers between devices: 107 us -> 180 us
  local copies, waits for them, and re-layouts: 14.2 us -> 53.7 us
  other arithmetic: 8.11 us -> 18.7 us
  starting transfers between devices: 6.49 us -> 13.7 us
    psum x1 -> x4, waiting for transfers between devices: 56.7 us -> 150 us  [reduce_pending(): total = lax.psum(pending, 'sta')]
    conv_general_dilated x1 -> x4, matrix products: 18.6 us -> 110 us  [body(): lax.conv_general_dilated(received, template, (1,), 'VALID', dimension_num...]
    all_to_all x1 -> x3, waiting for transfers between devices: 50 us -> 28.6 us  [body(): lax.all_to_all(sending, 'evt', split_axis=0, concat_axis=0, tiled=True)]
    all_to_all x0 -> x1, blocking collectives: none -> 20.3 us  [body(): lax.all_to_all(sending, 'evt', split_axis=0, concat_axis=0, tiled=True)]
    psum x1 -> x0, blocking collectives: 18.1 us -> none  [body(): lax.psum((lag_scores, slot_energy, event_energy), 'sta')]
    another operation x0 -> x4, local copies, waits for them, and re-layouts: none -> 8.08 us  [body(): jnp.stack(outs, axis=0).reshape(chunks, events, lag_count, devices_evt, per)]
    reshape x1 -> x3, local copies, waits for them, and re-layouts: 2.74 us -> 10.7 us  [the longest x1 5.25 us: body(): jnp.transpose(coef, (1, 2, 3, 0, 4)).reshape(events, lag_count, slot_count)]
    slice x0 -> x6, local copies, waits for them, and re-layouts: none -> 7.24 us  [the longest x3 3.89 us: reduce_pending(): parts[-1] = (previous[:events], previous[events])]
  transfers between devices with their start and end apart: 2 -> 7, of which waited for: 2 -> 6; matrix products, arithmetic and copies ran while one was open for 5% -> 19% of each run, Pallas kernels for 0% -> 0%
where the time goes in v1:
time: 418 us; the launch traced here: 411 us
  waiting for transfers between devices  180 us (43%)
  matrix products  111 us (27%)
  local copies, waits for them, and re-layouts  53.7 us (13%)
  blocking collectives  20.3 us (5%)
  other arithmetic  18.7 us (4%)
  between operations  13.9 us (3%)
  starting transfers between devices  13.7 us (3%)
    psum x4, waiting for transfers between devices, reduce_pending(): total = lax.psum(pending, 'sta')  150 us
    conv_general_dilated x4, matrix products, body(): lax.conv_general_dilated(received, template, (1,), 'VALID', dimension_num...  110 us
    all_to_all x3, waiting for transfers between devices, body(): lax.all_to_all(sending, 'evt', split_axis=0, concat_axis=0, tiled=True)  28.6 us
    all_to_all x1, blocking collectives, body(): lax.all_to_all(sending, 'evt', split_axis=0, concat_axis=0, tiled=True)  20.3 us
    all_to_all x3, starting transfers between devices, body(): lax.all_to_all(sending, 'evt', split_axis=0, concat_axis=0, tiled=True)  13.5 us
    all_to_all x4, local copies, waits for them, and re-layouts, body(): lax.all_to_all(sending, 'evt', split_axis=0, concat_axis=0, tiled=True)  12.5 us
  transfers between devices with their start and end apart: 7, of which 6 were waited for; matrix products, arithmetic and copies ran while one was open for 19% of the time, Pallas kernels for 0%

profile of v1, /device:TPU:0, one launch (start us, length us, event | category | flops | bytes accessed | tf_op | source)
XLA Modules:
  0.0 411.5 jit_solution(14896882633229301000)
XLA Ops:
  6.5 0.8 copy.46
  7.3 0.1 reshape.56
  7.4 0.1 fusion.5
  7.5 0.2 reduce_window_sum.11
  7.7 0.2 select_reduce_fusion
  7.9 2.1 reshape.57
  10.0 0.9 convolution_convert_fusion
  10.9 2.7 copy.47
  13.6 4.2 %reshape.58 = bf16[8,4,4,24,280]{4,3,2,1,0:T(8,128)(2,1)S(1)} reshape(bf16[128,6720]{1,0:T(8,128)(2,1)} %copy.47) | data formatting | bytes 3440640 | tf_op jit(solution)/shard_map/reshape | solution.py:45
  17.9 1.5 fusion.10
  19.4 6.5 %all-to-all-start = ((bf16[32,24,280]{2,1,0:T(8,128)(2,1)}), bf16[32,24,280]{2,1,0:T(8,128)(2,1)S(1)}, u32[]{:S(2)}, u32[]{:S(2)}) async-start(bf16[32,24,280]{2,1,0:T(8,128)(2,1)} %bitcast), calls=%async_computation | async-start | bytes 1179648 | tf_op jit(solution)/shard_map/all_to_all | solution.py:71
  25.9 1.0 multiply_reduce_fusion
  26.8 1.8 copy.49
  28.7 1.2 reshape.61
  29.9 12.7 %all-to-all-done = bf16[32,24,280]{2,1,0:T(8,128)(2,1)S(1)} async-done(((bf16[32,24,280]{2,1,0:T(8,128)(2,1)}), bf16[32,24,280]{2,1,0:T(8,128)(2,1)S(1)}, u32[]{:S(2)}, u32[]{:S(2)}) %all-to-all-start) | async-done | bytes 430112 | tf_op jit(solution)/shard_map/all_to_all | solution.py:71
  42.6 0.3 multiply_reduce_fusion.4
  42.9 0.2 convolution_bitcast_fusion.3
  43.1 1.3 copy.51
  44.3 3.4 copy.48
  47.8 28.2 %fusion.12 = f32[64,81,32]{0,2,1:T(8,128)S(1)} fusion(bf16[32,24,280]{0,1,2:T(8,128)(2,1)} %copy.48, bf16[64,24,200]{0,1,2:T(8,128)(2,1)} %copy.49), kind=kOutput, calls=%fused_computation.40 | convolution fusion | flops 1592524800 | bytes 1708032 | tf_op jit(solution)/shard_map/conv_general_dilated | solution.py:74
  76.0 1.8 pad_maximum_fusion.1
  77.8 20.3 %all_to_all.20 = bf16[32,24,280]{2,1,0:T(8,128)(2,1)S(1)} all-to-all(bf16[32,24,280]{2,1,0:T(8,128)(2,1)} %bitcast.45), channel_id=1, replica_groups=mesh['sta'=4,'evt'=8] {'evt'}, dimensions={0} | all-to-all | bytes 860160 | tf_op jit(solution)/shard_map/all_to_all | solution.py:71
  98.2 0.3 multiply_reduce_fusion.3
  98.5 0.2 convolution_bitcast_fusion.2
  98.6 2.9 copy.53
  101.6 27.2 %fusion.13 = f32[64,81,32]{0,2,1:T(8,128)} fusion(bf16[32,24,280]{0,1,2:T(8,128)(2,1)S(1)} %copy.53, bf16[64,24,200]{0,1,2:T(8,128)(2,1)S(1)} %copy-done.7), kind=kOutput, calls=%fused_computation.41 | convolution fusion | flops 1592524800 | bytes 1708032 | tf_op jit(solution)/shard_map/conv_general_dilated | solution.py:74
  128.8 1.3 copy.56
  130.1 1.5 pad_maximum_fusion.2
  131.6 3.5 all-to-all-start.2
  135.2 0.7 all-reduce.6.cloned.1.call-update
  135.9 15.9 %all-to-all-done.2 = bf16[32,24,280]{2,1,0:T(8,128)(2,1)S(1)} async-done(((bf16[32,24,280]{2,1,0:T(8,128)(2,1)}), bf16[32,24,280]{2,1,0:T(8,128)(2,1)S(1)}, u32[]{:S(2)}, u32[]{:S(2)}) %all-to-all-start.2) | async-done | bytes 430112 | tf_op jit(solution)/shard_map/all_to_all | solution.py:71
  151.8 3.1 copy.59
  155.0 27.2 %fusion.14 = f32[64,81,32]{0,2,1:T(8,128)} fusion(bf16[32,24,280]{0,1,2:T(8,128)(2,1)S(1)} %copy.59, bf16[64,24,200]{0,1,2:T(8,128)(2,1)S(1)} %copy-done.8), kind=kOutput, calls=%fused_computation.42 | convolution fusion | flops 1592524800 | bytes 1708032 | tf_op jit(solution)/shard_map/conv_general_dilated | solution.py:74
  182.2 0.3 multiply_reduce_fusion.2
  182.5 0.2 convolution_bitcast_fusion.1
  182.6 1.3 copy.62
  183.9 1.5 pad_maximum_fusion.3
  185.4 3.6 all-to-all-start.3
  189.0 8.5 %all-reduce.6.cloned.1.call-done = f32[66,81,32]{0,2,1:T(8,128)} async-done(((f32[66,81,32]{0,2,1:T(8,128)}), f32[66,81,32]{0,2,1:T(8,128)}) %all-reduce.6.cloned.1.call-update) | async-done | bytes 684304 | tf_op jit(solution)/shard_map/psum | solution.py:61
  197.6 60.6 %all-reduce.8.cloned.1.call-done = f32[65,81,32]{0,2,1:T(8,128)} async-done(((f32[65,81,32]{0,2,1:T(8,128)}), f32[65,81,32]{0,2,1:T(8,128)}) %all-reduce.8.cloned.1.call-update) | async-done | bytes 673936 | tf_op jit(solution)/shard_map/psum | solution.py:61
  258.2 3.0 copy.65
  261.2 27.2 %fusion.15 = f32[64,81,32]{0,2,1:T(8,128)} fusion(bf16[32,24,280]{0,1,2:T(8,128)(2,1)S(1)} %copy.65, bf16[64,24,200]{0,1,2:T(8,128)(2,1)S(1)} %copy-done.9), kind=kOutput, calls=%fused_computation.43 | convolution fusion | flops 1592524800 | bytes 1708032 | tf_op jit(solution)/shard_map/conv_general_dilated | solution.py:74
  288.4 0.3 multiply_reduce_fusion.1
  288.7 0.2 convolution_bitcast_fusion
  288.9 1.3 copy.68
  290.2 1.5 pad_maximum_fusion.4
  291.7 26.8 %all-reduce.10.cloned.1.call-done = f32[65,81,32]{0,2,1:T(8,128)} async-done(((f32[65,81,32]{0,2,1:T(8,128)}), f32[65,81,32]{0,2,1:T(8,128)}) %all-reduce.10.cloned.1.call-update) | async-done | bytes 673936 | tf_op jit(solution)/shard_map/psum | solution.py:61
  318.5 0.2 slice_reduce_fusion
  318.7 0.4 slice.51
  319.2 0.6 copy.78
  319.7 1.7 slice.54
  321.5 0.6 copy.79
  322.1 1.7 slice.56
  323.8 0.6 copy.80
  324.4 54.6 %all-reduce.12.cloned.1.call-done = f32[65,81,32]{0,2,1:T(8,128)} async-done(((f32[65,81,32]{0,2,1:T(8,128)}), f32[65,81,32]{0,2,1:T(8,128)}) %all-reduce.12.cloned.1.call-update) | async-done | bytes 673936 | tf_op jit(solution)/shard_map/psum | solution.py:61
  378.9 1.7 slice.65
  380.7 0.6 copy.81
  381.3 5.3 %rsqrt_multiply_fusion.2 = (f32[64,81,32]{0,2,1:T(8,128)}, f32[64,81,32]{0,2,1:T(8,128)}, f32[64,81,32]{0,2,1:T(8,128)}, f32[64,81,32]{0,2,1:T(8,128)S(1)}) fusion(f32[66,81,32]{0,2,1:T(8,128)S(1)} %copy-done, f32[81,32]{1,0:T(8,128)S(1)} %bitcast.46, f32[64]{0:T(128)S(1)} %mul.111, f32[81,32]{1,0:T(8,128)S(1)} %bitcast.47, ...), kind=kLoop, calls=%fused_computation.10 | loop fusion | flops 1990656 | bytes 5350144 | tf_op jit(solution)/shard_map/div | solution.py:98
  386.6 2.5 copy.73
  389.1 2.6 copy.74
  391.7 1.5 copy.75
  393.2 1.5 copy.76
  394.7 4.5 %pad_maximum_fusion = f32[4,64,81,8,4]{2,1,4,0,3:T(8,128)} fusion(f32[1,64,81,8,4]{2,1,4,0,3:T(8,128)} %copy.76, f32[1,64,81,8,4]{2,1,4,0,3:T(8,128)} %copy.75, f32[1,64,81,8,4]{2,1,4,0,3:T(8,128)} %copy.74, f32[1,64,81,8,4]{2,1,4,0,3:T(8,128)S(1)} %copy-done.2), kind=kLoop, calls=%fused_computation.1 | loop fusion | flops 1990656 | bytes 5308416 | tf_op jit(solution)/shard_map/stack | solution.py:101
  399.2 5.2 %copy.77 = f32[64,81,128]{2,0,1:T(8,128)} copy(f32[64,81,128]{1,0,2:T(8,128)} %bitcast.40) | data formatting | bytes 5308416 | tf_op jit(solution)/shard_map/reshape | solution.py:102
  (45 shorter events, 0.4 us)
Async XLA Ops:
  17.9 7.9 %copy-start.12 = (s32[24]{0:T(128)S(1)}, s32[24]{0:T(128)}, u32[]{:S(2)}) copy-start(s32[24]{0:T(128)} %param.4) | copy-start | bytes 292
  19.4 6.5 %copy-start.3 = (bf16[64,24,280]{2,1,0:T(8,128)(2,1)S(1)}, bf16[64,24,280]{2,1,0:T(8,128)(2,1)}, u32[]{:S(2)}) copy-start(bf16[64,24,280]{2,1,0:T(8,128)(2,1)} %param.3) | copy-start | bytes 2580484
  19.4 23.2 %all-to-all-start = ((bf16[32,24,280]{2,1,0:T(8,128)(2,1)}), bf16[32,24,280]{2,1,0:T(8,128)(2,1)S(1)}, u32[]{:S(2)}, u32[]{:S(2)}) async-start(bf16[32,24,280]{2,1,0:T(8,128)(2,1)} %bitcast), calls=%async_computation | async-start | bytes 1179648 | tf_op jit(solution)/shard_map/all_to_all | solution.py:71
  25.8 72.3 %copy-start.10 = (f32[24]{0:T(128)}, f32[24]{0:T(128)S(1)}, u32[]{:S(2)}) copy-start(f32[24]{0:T(128)S(1)} %get-tuple-element.39) | copy-start | bytes 292
  29.9 13.0 %copy-start.13 = (s32[81]{0:T(128)}, s32[81]{0:T(128)S(1)}, u32[]{:S(2)}) copy-start(s32[81]{0:T(128)S(1)} %iota_add_fusion) | copy-start | bytes 976
  77.8 20.6 %copy-start.14 = (s32[81]{0:T(128)S(1)}, s32[81]{0:T(128)}, u32[]{:S(2)}) copy-start(s32[81]{0:T(128)} %copy-done.13) | copy-start | bytes 976
  98.4 3.1 copy-start.7
  128.8 1.3 copy-start.6
  131.6 20.2 %all-to-all-start.2 = ((bf16[32,24,280]{2,1,0:T(8,128)(2,1)}), bf16[32,24,280]{2,1,0:T(8,128)(2,1)S(1)}, u32[]{:S(2)}, u32[]{:S(2)}) async-start(bf16[32,24,280]{2,1,0:T(8,128)(2,1)} %bitcast.4), calls=%async_computation.2 | async-start | bytes 1179648 | tf_op jit(solution)/shard_map/all_to_all | solution.py:71
  135.1 62.4 %all-reduce.6.cloned.1.call-start = ((), (), s32[]{:S(2)}) async-start(), calls=%async_computation.4 | async-start | bytes 2654208 | tf_op jit(solution)/shard_map/psum | solution.py:61
  135.9 19.1 %copy-start.8 = (bf16[64,24,200]{0,1,2:T(8,128)(2,1)S(1)}, bf16[64,24,200]{0,1,2:T(8,128)(2,1)}, u32[]{:S(2)}) copy-start(bf16[64,24,200]{0,1,2:T(8,128)(2,1)} %copy.49) | copy-start | bytes 1843204
  155.0 27.2 %copy-start.11 = (f32[24]{0:T(128)S(1)}, f32[24]{0:T(128)}, u32[]{:S(2)}) copy-start(f32[24]{0:T(128)} %copy-done.10) | copy-start | bytes 292
  155.0 27.5 %copy-start.15 = (s32[81]{0:T(128)S(1)}, s32[81]{0:T(128)}, u32[]{:S(2)}) copy-start(s32[81]{0:T(128)} %copy-done.13) | copy-start | bytes 976
  182.2 1.8 copy-start.5
  185.4 72.8 %all-to-all-start.3 = ((bf16[32,24,280]{2,1,0:T(8,128)(2,1)}), bf16[32,24,280]{2,1,0:T(8,128)(2,1)S(1)}, u32[]{:S(2)}, u32[]{:S(2)}) async-start(bf16[32,24,280]{2,1,0:T(8,128)(2,1)} %bitcast.9), calls=%async_computation.3 | async-start | bytes 1179648 | tf_op jit(solution)/shard_map/all_to_all | solution.py:71
  189.0 69.2 %all-reduce.8.cloned.1.call-start = ((), (), s32[]{:S(2)}) async-start(), calls=%async_computation.5 | async-start | bytes 2654208 | tf_op jit(solution)/shard_map/psum | solution.py:61
  197.5 120.9 %all-reduce.10.cloned.1.call-start = ((), (), s32[]{:S(2)}) async-start(), calls=%async_computation.6 | async-start | bytes 2654208 | tf_op jit(solution)/shard_map/psum | solution.py:61
  258.2 3.1 copy-start.9
  258.2 120.8 %all-reduce.12.cloned.1.call-start = ((), (), s32[]{:S(2)}) async-start(), calls=%async_computation.7 | async-start | bytes 2654208 | tf_op jit(solution)/shard_map/psum | solution.py:61
  288.4 1.8 copy-start.4
  291.7 26.8 %copy-start = (f32[66,81,32]{0,2,1:T(8,128)S(1)}, f32[66,81,32]{0,2,1:T(8,128)}, u32[]{:S(2)}) copy-start(f32[66,81,32]{0,2,1:T(8,128)} %all-reduce.6.cloned.1.call-done) | copy-start | bytes 2052868
  389.1 2.6 copy-start.1
  393.2 1.5 copy-start.2
Sparse Core Ops, SparseCore 0:
  139.1 58.3 all-reduce.5
  200.9 57.1 all-reduce.7
  261.3 57.1 all-reduce.9
  321.7 57.1 all-reduce.11

commit v2 on v0

--- a/solution.py
+++ b/solution.py
@@ -17,10 +17,49 @@
     return lag_scores / jnp.sqrt(event_energy[:, None, None] * slot_energy[None, :, :] + 1e-06)
 
 
+def exchange(value, axis, bit, size):
+    return lax.ppermute(value, axis, [(i, i ^ bit) for i in range(size)])
+
+
+def pick(pair, upper):
+    return jnp.where(upper, pair[1], pair[0]), jnp.where(upper, pair[0], pair[1])
+
+
+def place(mine, other, upper):
+    return jnp.where(upper, jnp.stack([other, mine]), jnp.stack([mine, other]))
+
+
+def halving_allreduce(data, axis, bits):
+    size = lax.axis_size(axis)
+    index = lax.axis_index(axis)
+    uppers = [(index & bit) != 0 for bit in bits]
+    acc = data
+    for bit, upper in zip(bits, uppers):
+        acc = acc.reshape((2, acc.shape[0] // 2) + acc.shape[1:])
+        keep, send = pick(acc, upper)
+        acc = keep + exchange(send, axis, bit, size)
+    for bit, upper in zip(bits[::-1], uppers[::-1]):
+        acc = place(acc, exchange(acc, axis, bit, size), upper)
+        acc = acc.reshape((-1,) + acc.shape[2:])
+    return acc
+
+
+def sta_allreduce(data):
+    size = lax.axis_size("sta")
+    if size & (size - 1) or size == 1:
+        return lax.psum(data, "sta")
+    bits = [1 << k for k in range(size.bit_length() - 1)]
+    half = data.shape[0] // 2
+    first = halving_allreduce(data[:half], "sta", bits)
+    second = halving_allreduce(data[half:], "sta", bits[::-1])
+    return jnp.concatenate([first, second], axis=0)
+
+
 def body(traces, channel_valid, partner_block):
     events, channels, extent = traces.shape
     partners = partner_block.shape[1]
     devices_evt = lax.axis_size("evt")
+    sta_size = lax.axis_size("sta")
     capacity = max(2, (events * partners + devices_evt - 1) // devices_evt)
     slot_count = devices_evt * capacity
     lag_count = extent - WIN + 1
@@ -72,8 +111,14 @@
         (((0,), (1,)), ((), ())),
         precision=lax.Precision.HIGHEST,
     )
-    scores_all, slot_all, event_all = lax.psum((lag_scores, slot_energy, event_energy), "sta")
-    return normalize(scores_all, slot_all, event_all)
+    extra = 2 * sta_size
+    pad = jnp.zeros((lag_count * slot_count - events,), jnp.float32)
+    energy_row = jnp.concatenate([event_energy, pad]).reshape(1, lag_count, slot_count)
+    filler = jnp.zeros((extra - 2, lag_count, slot_count), jnp.float32)
+    packed = jnp.concatenate([lag_scores, slot_energy[None], energy_row, filler], axis=0)
+    total = sta_allreduce(packed)
+    event_all = total[events + 1].reshape(-1)[:events]
+    return normalize(total[:events], total[events], event_all)
 
 
 def solution(mesh):

time: 187 us -> 183 us (0.979)
  blocking collectives: 18.1 us -> 0 us
  waiting for transfers between devices: 107 us -> 124 us
  between operations: 13.5 us -> 0.24 us
  starting transfers between devices: 6.49 us -> 15.3 us
  local copies, waits for them, and re-layouts: 14.2 us -> 17.7 us
    ppermute x0 -> x8, waiting for transfers between devices: none -> 74.6 us  [exchange(): return lax.ppermute(value, axis, [(i, i ^ bit) for i in range(size)])]
    psum x1 -> x0, waiting for transfers between devices: 56.7 us -> none  [body(): lax.psum((lag_scores, slot_energy, event_energy), 'sta')]
    psum x1 -> x0, blocking collectives: 18.1 us -> none  [body(): lax.psum((lag_scores, slot_energy, event_energy), 'sta')]
    ppermute x0 -> x8, starting transfers between devices: none -> 8.83 us  [exchange(): return lax.ppermute(value, axis, [(i, i ^ bit) for i in range(size)])]
    div x1, other arithmetic: 3.95 us -> 0.45 us  [normalize(): lag_scores / jnp.sqrt(event_energy[:, None, None] * slot_energy[None, :,...]
    div x0 -> x1, local copies, waits for them, and re-layouts: none -> 1.98 us  [normalize(): lag_scores / jnp.sqrt(event_energy[:, None, None] * slot_energy[None, :,...]
  transfers between devices with their start and end apart: 2 -> 9, of which waited for: 2 -> 8; matrix products, arithmetic and copies ran while one was open for 5% -> 3% of each run, Pallas kernels for 0% -> 0%
where the time goes in v2:
time: 183 us
  waiting for transfers between devices  124 us (68%)
  matrix products  18.4 us (10%)
  local copies, waits for them, and re-layouts  17.7 us (10%)
  starting transfers between devices  15.3 us (8%)
  other arithmetic  6.78 us (4%)
    ppermute x8, waiting for transfers between devices, exchange(): return lax.ppermute(value, axis, [(i, i ^ bit) for i in range(size)])  74.6 us
    all_to_all x1, waiting for transfers between devices, body(): lax.all_to_all(outgoing.reshape(slot_count, channels, extent), 'evt', spl...  49.8 us
    conv_general_dilated x1, matrix products, body(): lax.conv_general_dilated(received, template, (1,), 'VALID', dimension_num...  17.2 us
    ppermute x8, starting transfers between devices, exchange(): return lax.ppermute(value, axis, [(i, i ^ bit) for i in range(size)])  8.83 us
    all_to_all x1, starting transfers between devices, body(): lax.all_to_all(outgoing.reshape(slot_count, channels, extent), 'evt', spl...  6.46 us
    all_to_all x2, local copies, waits for them, and re-layouts, body(): lax.all_to_all(outgoing.reshape(slot_count, channels, extent), 'evt', spl...  5.44 us
  transfers between devices with their start and end apart: 9, of which 8 were waited for; matrix products, arithmetic and copies ran while one was open for 3% of the time, Pallas kernels for 0%

profile of v2, /device:TPU:0, one launch (start us, length us, event | category | flops | bytes accessed | tf_op | source)
XLA Modules:
  0.0 182.9 jit_solution(17894149403400494842)
XLA Ops:
  0.0 0.8 copy.59
  0.8 0.1 reshape.120
  0.9 0.1 fusion.6
  1.0 0.2 reduce_window_sum.11
  1.2 0.2 select_reduce_fusion
  1.4 2.1 %reshape.121 = bf16[64,6720]{1,0:T(8,128)(2,1)S(1)} reshape(bf16[64,24,280]{2,1,0:T(8,128)(2,1)} %param.3) | data formatting | bytes 1720320 | tf_op jit(solution)/shard_map/reshape | solution.py:84
  3.5 0.9 convolution_convert_fusion
  4.4 2.7 %copy.60 = bf16[128,24,280]{2,1,0:T(8,128)(2,1)} copy(bf16[128,24,280]{0,2,1:T(8,128)(2,1)S(1)} %bitcast.25) | data formatting | bytes 3440640 | tf_op jit(solution)/shard_map/reshape | solution.py:87
  7.2 0.0 copy-start.1
  7.2 0.0 copy-start
  7.2 6.5 %all-to-all-start = ((bf16[128,24,280]{2,1,0:T(8,128)(2,1)}), bf16[128,24,280]{2,1,0:T(8,128)(2,1)S(1)}, u32[]{:S(2)}, u32[]{:S(2)}) async-start(bf16[128,24,280]{2,1,0:T(8,128)(2,1)} %copy.60), calls=%async_computation | async-start | bytes 4718592 | tf_op jit(solution)/shard_map/all_to_all | solution.py:86
  13.6 0.0 copy-done.1
  13.6 0.0 copy-done
  13.6 1.8 %multiply_reduce_fusion.1 = (f32[64]{0:T(128)S(1)}, bf16[64,24,200]{2,1,0:T(8,128)(2,1)}) fusion(bf16[24]{0:T(256)(128)(2,1)S(1)} %get-tuple-element.14, bf16[64,24,280]{2,1,0:T(8,128)(2,1)S(1)} %copy-done), kind=kLoop, calls=%fused_computation.6 | loop fusion | flops 1228736 | bytes 1229104 | tf_op jit(solution)/shard_map/reduce_sum | solution.py:103
  15.5 2.9 %copy.62 = bf16[64,24,200]{0,1,2:T(8,128)(2,1)} copy(bf16[64,24,200]{2,1,0:T(8,128)(2,1)} %get-tuple-element.6) | data formatting | bytes 1228800 | tf_op jit(solution)/shard_map/mul | solution.py:94
  18.4 0.1 pad_slice_fusion
  18.5 49.8 %all-to-all-done = bf16[128,24,280]{2,1,0:T(8,128)(2,1)S(1)} async-done(((bf16[128,24,280]{2,1,0:T(8,128)(2,1)}), bf16[128,24,280]{2,1,0:T(8,128)(2,1)S(1)}, u32[]{:S(2)}, u32[]{:S(2)}) %all-to-all-start) | async-done | bytes 1720352 | tf_op jit(solution)/shard_map/all_to_all | solution.py:86
  68.3 2.6 %copy.71 = bf16[128,24,280]{0,2,1:T(8,128)(2,1)} copy(bf16[128,24,280]{2,1,0:T(8,128)(2,1)S(1)} %all-to-all-done) | data formatting | bytes 3440640 | tf_op jit(solution)/shard_map/all_to_all | solution.py:86
  70.9 1.9 %multiply_reduce_fusion = f32[128,280]{0,1:T(8,128)S(1)} fusion(bf16[128,24,280]{0,2,1:T(8,128)(2,1)} %copy.71, f32[24]{0:T(128)S(1)} %get-tuple-element.13), kind=kLoop, calls=%fused_computation.1 | loop fusion | flops 3404800 | bytes 1863776 | tf_op jit(solution)/shard_map/reduce_sum | solution.py:104
  72.8 0.3 fusion.3
  73.2 2.9 %copy.61 = bf16[128,24,280]{0,1,2:T(8,128)(2,1)} copy(bf16[128,24,280]{2,1,0:T(8,128)(2,1)S(1)} %all-to-all-done) | data formatting | bytes 3440640 | tf_op jit(solution)/shard_map/all_to_all | solution.py:86
  76.1 17.2 %fusion.12 = f32[64,81,128]{2,0,1:T(8,128)S(1)} fusion(bf16[128,24,280]{0,1,2:T(8,128)(2,1)} %copy.61, bf16[64,24,200]{0,1,2:T(8,128)(2,1)} %copy.62), kind=kOutput, calls=%fused_computation.46 | convolution fusion | flops 6370099200 | bytes 4988928 | tf_op jit(solution)/shard_map/conv_general_dilated | solution.py:95
  93.2 0.5 slice_select_fusion.1
  93.7 0.2 copy.63
  93.9 0.2 copy.73
  94.1 1.6 collective-permute-start.4
  95.7 1.5 collective-permute-start
  97.1 16.6 %collective-permute-done.4 = f32[18,81,128]{2,1,0:T(8,128)S(1)} collective-permute-done((f32[18,81,128]{2,1,0:T(8,128)S(1)}, f32[18,81,128]{2,1,0:T(8,128)S(1)}, u32[]{:S(2)}, u32[]{:S(2)}) %collective-permute-start.4) | collective-permute-done | bytes 746528 | tf_op jit(solution)/shard_map/ppermute | solution.py:21
  113.7 1.2 collective-permute-done
  115.0 0.7 copy_add_fusion.1
  115.7 0.1 slice_select_fusion.2
  115.8 0.1 copy.75
  116.0 1.6 collective-permute-start.5
  117.5 8.2 %collective-permute-done.5 = f32[9,81,128]{2,1,0:T(8,128)S(1)} collective-permute-done((f32[9,81,128]{2,1,0:T(8,128)S(1)}, f32[9,81,128]{2,1,0:T(8,128)S(1)}, u32[]{:S(2)}, u32[]{:S(2)}) %collective-permute-start.5) | collective-permute-done | bytes 373280 | tf_op jit(solution)/shard_map/ppermute | solution.py:21
  125.7 0.2 copy_add_fusion.2
  125.9 0.1 copy.77
  126.0 1.5 collective-permute-start.6
  127.6 0.1 slice_select_fusion.3
  127.7 0.1 copy.65
  127.8 0.7 collective-permute-start.1
  128.4 6.5 %collective-permute-done.6 = f32[9,81,128]{2,1,0:T(8,128)S(1)} collective-permute-done((f32[9,81,128]{2,1,0:T(8,128)S(1)}, f32[9,81,128]{2,1,0:T(8,128)S(1)}, u32[]{:S(2)}, u32[]{:S(2)}) %collective-permute-start.6) | collective-permute-done | bytes 373280 | tf_op jit(solution)/shard_map/ppermute | solution.py:21
  134.9 0.1 copy.89
  135.0 0.1 maximum_select_fusion.3
  135.1 0.2 copy.79
  135.4 0.7 collective-permute-start.7
  136.1 2.0 %collective-permute-done.1 = f32[9,81,128]{2,1,0:T(8,128)S(1)} collective-permute-done((f32[9,81,128]{2,1,0:T(8,128)S(1)}, f32[9,81,128]{2,1,0:T(8,128)S(1)}, u32[]{:S(2)}, u32[]{:S(2)}) %collective-permute-start.1) | collective-permute-done | bytes 373280 | tf_op jit(solution)/shard_map/ppermute | solution.py:21
  138.1 0.2 copy_add_fusion.3
  138.2 0.1 copy.67
  138.4 0.7 collective-permute-start.2
  139.0 23.4 %collective-permute-done.2 = f32[9,81,128]{2,1,0:T(8,128)S(1)} collective-permute-done((f32[9,81,128]{2,1,0:T(8,128)S(1)}, f32[9,81,128]{2,1,0:T(8,128)S(1)}, u32[]{:S(2)}, u32[]{:S(2)}) %collective-permute-start.2) | collective-permute-done | bytes 373280 | tf_op jit(solution)/shard_map/ppermute | solution.py:21
  162.4 0.1 copy.90
  162.6 0.1 maximum_select_fusion.2
  162.7 0.2 copy.69
  162.9 0.6 collective-permute-start.3
  163.5 0.0 collective-permute-done.7
  163.5 0.1 maximum_select_fusion.1
  163.7 16.7 %collective-permute-done.3 = f32[18,81,128]{2,1,0:T(8,128)S(1)} collective-permute-done((f32[18,81,128]{2,1,0:T(8,128)S(1)}, f32[18,81,128]{2,1,0:T(8,128)S(1)}, u32[]{:S(2)}, u32[]{:S(2)}) %collective-permute-start.3) | collective-permute-done | bytes 746528 | tf_op jit(solution)/shard_map/ppermute | solution.py:21
  180.4 0.1 maximum_select_fusion
  180.5 0.5 fusion
  180.9 2.0 %copy.81 = f32[64,81,128]{2,0,1:T(8,128)} copy(f32[64,81,128]{2,1,0:T(8,128)S(1)} %fusion) | data formatting | bytes 5308416 | tf_op jit(solution)/shard_map/div | solution.py:17
  (9 shorter events, 0.1 us)
Async XLA Ops:
  7.2 6.5 %copy-start.1 = (s32[24]{0:T(128)S(1)}, s32[24]{0:T(128)}, u32[]{:S(2)}) copy-start(s32[24]{0:T(128)} %param.4) | copy-start | bytes 292
  7.2 6.5 %copy-start = (bf16[64,24,280]{2,1,0:T(8,128)(2,1)S(1)}, bf16[64,24,280]{2,1,0:T(8,128)(2,1)}, u32[]{:S(2)}) copy-start(bf16[64,24,280]{2,1,0:T(8,128)(2,1)} %param.3) | copy-start | bytes 2580484
  7.2 61.1 %all-to-all-start = ((bf16[128,24,280]{2,1,0:T(8,128)(2,1)}), bf16[128,24,280]{2,1,0:T(8,128)(2,1)S(1)}, u32[]{:S(2)}, u32[]{:S(2)}) async-start(bf16[128,24,280]{2,1,0:T(8,128)(2,1)} %copy.60), calls=%async_computation | async-start | bytes 4718592 | tf_op jit(solution)/shard_map/all_to_all | solution.py:86
  94.1 19.7 %collective-permute-start.4 = (f32[18,81,128]{2,1,0:T(8,128)S(1)}, f32[18,81,128]{2,1,0:T(8,128)S(1)}, u32[]{:S(2)}, u32[]{:S(2)}) collective-permute-start(f32[18,81,128]{2,1,0:T(8,128)S(1)} %copy.73), channel_id=1, source_target_pairs={{0,16},{8,24},{16,0},{24,8},{1,17},{9,25},{17,1},{25,9},{2,18},{10... | collective-permute-start | bytes 2239496 | tf_op jit(solution)/shard_map/ppermute | solution.py:21
  95.7 19.3 %collective-permute-start = (f32[18,81,128]{2,1,0:T(8,128)S(1)}, f32[18,81,128]{2,1,0:T(8,128)S(1)}, u32[]{:S(2)}, u32[]{:S(2)}) collective-permute-start(f32[18,81,128]{2,1,0:T(8,128)S(1)} %copy.63), channel_id=1, source_target_pairs={{0,8},{8,0},{16,24},{24,16},{1,9},{9,1},{17,25},{25,17},{2,10},{10... | collective-permute-start | bytes 2239496 | tf_op jit(solution)/shard_map/ppermute | solution.py:21
  116.0 9.8 %collective-permute-start.5 = (f32[9,81,128]{2,1,0:T(8,128)S(1)}, f32[9,81,128]{2,1,0:T(8,128)S(1)}, u32[]{:S(2)}, u32[]{:S(2)}) collective-permute-start(f32[9,81,128]{2,1,0:T(8,128)S(1)} %copy.75), channel_id=1, source_target_pairs={{0,8},{8,0},{16,24},{24,16},{1,9},{9,1},{17,25},{25,17},{2,10},{10... | collective-permute-start | bytes 1119752 | tf_op jit(solution)/shard_map/ppermute | solution.py:21
  126.0 8.9 %collective-permute-start.6 = (f32[9,81,128]{2,1,0:T(8,128)S(1)}, f32[9,81,128]{2,1,0:T(8,128)S(1)}, u32[]{:S(2)}, u32[]{:S(2)}) collective-permute-start(f32[9,81,128]{2,1,0:T(8,128)S(1)} %copy.77), channel_id=1, source_target_pairs={{0,8},{8,0},{16,24},{24,16},{1,9},{9,1},{17,25},{25,17},{2,10},{10... | collective-permute-start | bytes 1119752 | tf_op jit(solution)/shard_map/ppermute | solution.py:21
  127.8 10.3 %collective-permute-start.1 = (f32[9,81,128]{2,1,0:T(8,128)S(1)}, f32[9,81,128]{2,1,0:T(8,128)S(1)}, u32[]{:S(2)}, u32[]{:S(2)}) collective-permute-start(f32[9,81,128]{2,1,0:T(8,128)S(1)} %copy.65), channel_id=1, source_target_pairs={{0,16},{8,24},{16,0},{24,8},{1,17},{9,25},{17,1},{25,9},{2,18},{10... | collective-permute-start | bytes 1119752 | tf_op jit(solution)/shard_map/ppermute | solution.py:21
  135.4 28.2 %collective-permute-start.7 = (f32[18,81,128]{2,1,0:T(8,128)S(1)}, f32[18,81,128]{2,1,0:T(8,128)S(1)}, u32[]{:S(2)}, u32[]{:S(2)}) collective-permute-start(f32[18,81,128]{2,1,0:T(8,128)S(1)} %bitcast.31), channel_id=1, source_target_pairs={{0,16},{8,24},{16,0},{24,8},{1,17},{9,25},{17,1},{25,9},{2,18},{10... | collective-permute-start | bytes 2239496 | tf_op jit(solution)/shard_map/ppermute | solution.py:21
  138.4 24.1 %collective-permute-start.2 = (f32[9,81,128]{2,1,0:T(8,128)S(1)}, f32[9,81,128]{2,1,0:T(8,128)S(1)}, u32[]{:S(2)}, u32[]{:S(2)}) collective-permute-start(f32[9,81,128]{2,1,0:T(8,128)S(1)} %copy.67), channel_id=1, source_target_pairs={{0,16},{8,24},{16,0},{24,8},{1,17},{9,25},{17,1},{25,9},{2,18},{10... | collective-permute-start | bytes 1119752 | tf_op jit(solution)/shard_map/ppermute | solution.py:21
  162.9 17.5 %collective-permute-start.3 = (f32[18,81,128]{2,1,0:T(8,128)S(1)}, f32[18,81,128]{2,1,0:T(8,128)S(1)}, u32[]{:S(2)}, u32[]{:S(2)}) collective-permute-start(f32[18,81,128]{2,1,0:T(8,128)S(1)} %bitcast.33), channel_id=1, source_target_pairs={{0,8},{8,0},{16,24},{24,16},{1,9},{9,1},{17,25},{25,17},{2,10},{10... | collective-permute-start | bytes 2239496 | tf_op jit(solution)/shard_map/ppermute | solution.py:21

commit v3 on v2

--- a/solution.py
+++ b/solution.py
@@ -29,30 +29,39 @@
     return jnp.where(upper, jnp.stack([other, mine]), jnp.stack([mine, other]))
 
 
-def halving_allreduce(data, axis, bits):
+def sta_allreduce(data):
+    axis = "sta"
     size = lax.axis_size(axis)
+    if size & (size - 1) or size == 1:
+        return lax.psum(data, axis)
     index = lax.axis_index(axis)
-    uppers = [(index & bit) != 0 for bit in bits]
-    acc = data
-    for bit, upper in zip(bits, uppers):
-        acc = acc.reshape((2, acc.shape[0] // 2) + acc.shape[1:])
-        keep, send = pick(acc, upper)
-        acc = keep + exchange(send, axis, bit, size)
-    for bit, upper in zip(bits[::-1], uppers[::-1]):
-        acc = place(acc, exchange(acc, axis, bit, size), upper)
-        acc = acc.reshape((-1,) + acc.shape[2:])
-    return acc
-
-
-def sta_allreduce(data):
-    size = lax.axis_size("sta")
-    if size & (size - 1) or size == 1:
-        return lax.psum(data, "sta")
     bits = [1 << k for k in range(size.bit_length() - 1)]
+    orders = [bits, bits[::-1]]
     half = data.shape[0] // 2
-    first = halving_allreduce(data[:half], "sta", bits)
-    second = halving_allreduce(data[half:], "sta", bits[::-1])
-    return jnp.concatenate([first, second], axis=0)
+    accs = [data[:half], data[half:]]
+    for stage in range(len(bits)):
+        sends, keeps = [], []
+        for h in range(2):
+            bit = orders[h][stage]
+            acc = accs[h].reshape((2, accs[h].shape[0] // 2) + accs[h].shape[1:])
+            keep, send = pick(acc, (index & bit) != 0)
+            sends.append(send)
+            keeps.append(keep)
+        sends = lax.optimization_barrier(sends)
+        got = [exchange(sends[h], axis, orders[h][stage], size) for h in range(2)]
+        got = lax.optimization_barrier(got)
+        accs = [keeps[h] + got[h] for h in range(2)]
+    for stage in reversed(range(len(bits))):
+        accs = lax.optimization_barrier(accs)
+        got = [exchange(accs[h], axis, orders[h][stage], size) for h in range(2)]
+        got = lax.optimization_barrier(got)
+        accs = [
+            place(accs[h], got[h], (index & orders[h][stage]) != 0).reshape(
+                (-1,) + accs[h].shape[1:]
+            )
+            for h in range(2)
+        ]
+    return jnp.concatenate(accs, axis=0)
 
 
 def body(traces, channel_valid, partner_block):

time: 183 us -> 158 us (0.86)
  waiting for transfers between devices: 124 us -> 99.3 us
    ppermute x8, waiting for transfers between devices: 74.6 us -> 49.5 us  [exchange(): return lax.ppermute(value, axis, [(i, i ^ bit) for i in range(size)])]
  transfers between devices with their start and end apart: 9 -> 9, of which waited for: 8 -> 9; matrix products, arithmetic and copies ran while one was open for 3% -> 3% of each run, Pallas kernels for 0% -> 0%
where the time goes in v3:
time: 158 us; the launch traced here: 157 us
  waiting for transfers between devices  99.3 us (63%)
  matrix products  18.4 us (12%)
  local copies, waits for them, and re-layouts  17.7 us (11%)
  starting transfers between devices  15 us (9%)
  other arithmetic  6.77 us (4%)
    all_to_all x1, waiting for transfers between devices, body(): lax.all_to_all(outgoing.reshape(slot_count, channels, extent), 'evt', spl...  49.8 us
    ppermute x8, waiting for transfers between devices, exchange(): return lax.ppermute(value, axis, [(i, i ^ bit) for i in range(size)])  49.5 us
    conv_general_dilated x1, matrix products, body(): lax.conv_general_dilated(received, template, (1,), 'VALID', dimension_num...  17.2 us
    ppermute x8, starting transfers between devices, exchange(): return lax.ppermute(value, axis, [(i, i ^ bit) for i in range(size)])  8.51 us
    all_to_all x1, starting transfers between devices, body(): lax.all_to_all(outgoing.reshape(slot_count, channels, extent), 'evt', spl...  6.46 us
    all_to_all x2, local copies, waits for them, and re-layouts, body(): lax.all_to_all(outgoing.reshape(slot_count, channels, extent), 'evt', spl...  5.44 us
  transfers between devices with their start and end apart: 9, of which 9 were waited for; matrix products, arithmetic and copies ran while one was open for 3% of the time, Pallas kernels for 0%

profile of v3, /device:TPU:0, one launch (start us, length us, event | category | flops | bytes accessed | tf_op | source)
XLA Modules:
  0.0 157.5 jit_solution(5706621561683570507)
XLA Ops:
  0.0 0.8 copy.53
  0.8 0.1 reshape.82
  0.9 0.1 fusion.6
  1.0 0.2 reduce_window_sum.11
  1.2 0.2 select_reduce_fusion
  1.4 2.1 %reshape.83 = bf16[64,6720]{1,0:T(8,128)(2,1)S(1)} reshape(bf16[64,24,280]{2,1,0:T(8,128)(2,1)} %param.3) | data formatting | bytes 1720320 | tf_op jit(solution)/shard_map/reshape | solution.py:93
  3.5 0.9 convolution_convert_fusion
  4.4 2.7 %copy.54 = bf16[128,24,280]{2,1,0:T(8,128)(2,1)} copy(bf16[128,24,280]{0,2,1:T(8,128)(2,1)S(1)} %bitcast.25) | data formatting | bytes 3440640 | tf_op jit(solution)/shard_map/reshape | solution.py:96
  7.2 0.0 copy-start.1
  7.2 0.0 copy-start
  7.2 6.5 %all-to-all-start = ((bf16[128,24,280]{2,1,0:T(8,128)(2,1)}), bf16[128,24,280]{2,1,0:T(8,128)(2,1)S(1)}, u32[]{:S(2)}, u32[]{:S(2)}) async-start(bf16[128,24,280]{2,1,0:T(8,128)(2,1)} %copy.54), calls=%async_computation | async-start | bytes 4718592 | tf_op jit(solution)/shard_map/all_to_all | solution.py:95
  13.6 0.0 copy-done.1
  13.6 0.0 copy-done
  13.6 1.8 %multiply_reduce_fusion.1 = (f32[64]{0:T(128)S(1)}, bf16[64,24,200]{2,1,0:T(8,128)(2,1)}) fusion(bf16[24]{0:T(256)(128)(2,1)S(1)} %get-tuple-element.46, bf16[64,24,280]{2,1,0:T(8,128)(2,1)S(1)} %copy-done), kind=kLoop, calls=%fused_computation.6 | loop fusion | flops 1228736 | bytes 1229104 | tf_op jit(solution)/shard_map/reduce_sum | solution.py:112
  15.5 2.9 %copy.56 = bf16[64,24,200]{0,1,2:T(8,128)(2,1)} copy(bf16[64,24,200]{2,1,0:T(8,128)(2,1)} %get-tuple-element.38) | data formatting | bytes 1228800 | tf_op jit(solution)/shard_map/mul | solution.py:103
  18.4 0.1 pad_slice_fusion
  18.5 49.8 %all-to-all-done = bf16[128,24,280]{2,1,0:T(8,128)(2,1)S(1)} async-done(((bf16[128,24,280]{2,1,0:T(8,128)(2,1)}), bf16[128,24,280]{2,1,0:T(8,128)(2,1)S(1)}, u32[]{:S(2)}, u32[]{:S(2)}) %all-to-all-start) | async-done | bytes 1720352 | tf_op jit(solution)/shard_map/all_to_all | solution.py:95
  68.3 2.6 %copy.57 = bf16[128,24,280]{0,2,1:T(8,128)(2,1)} copy(bf16[128,24,280]{2,1,0:T(8,128)(2,1)S(1)} %all-to-all-done) | data formatting | bytes 3440640 | tf_op jit(solution)/shard_map/all_to_all | solution.py:95
  70.9 1.9 %multiply_reduce_fusion = f32[128,280]{0,1:T(8,128)S(1)} fusion(bf16[128,24,280]{0,2,1:T(8,128)(2,1)} %copy.57, f32[24]{0:T(128)S(1)} %get-tuple-element.45), kind=kLoop, calls=%fused_computation.1 | loop fusion | flops 3404800 | bytes 1863776 | tf_op jit(solution)/shard_map/reduce_sum | solution.py:113
  72.8 0.3 fusion.3
  73.2 2.9 %copy.55 = bf16[128,24,280]{0,1,2:T(8,128)(2,1)} copy(bf16[128,24,280]{2,1,0:T(8,128)(2,1)S(1)} %all-to-all-done) | data formatting | bytes 3440640 | tf_op jit(solution)/shard_map/all_to_all | solution.py:95
  76.1 17.2 %fusion.12 = f32[64,81,128]{2,0,1:T(8,128)S(1)} fusion(bf16[128,24,280]{0,1,2:T(8,128)(2,1)} %copy.55, bf16[64,24,200]{0,1,2:T(8,128)(2,1)} %copy.56), kind=kOutput, calls=%fused_computation.46 | convolution fusion | flops 6370099200 | bytes 4988928 | tf_op jit(solution)/shard_map/conv_general_dilated | solution.py:104
  93.3 0.5 slice_select_fusion
  93.8 0.2 copy.59
  93.9 0.2 copy.60
  94.1 1.6 %collective-permute-start.1 = (f32[18,81,128]{2,1,0:T(8,128)S(1)}, f32[18,81,128]{2,1,0:T(8,128)S(1)}, u32[]{:S(2)}, u32[]{:S(2)}) collective-permute-start(f32[18,81,128]{2,1,0:T(8,128)S(1)} %copy.60), channel_id=1, source_target_pairs={{0,16},{8,24},{16,0},{24,8},{1,17},{9,25},{17,1},{25,9},{2,18},{10... | collective-permute-start | bytes 2239496 | tf_op jit(solution)/shard_map/ppermute | solution.py:21
  95.7 1.5 collective-permute-start
  97.2 16.6 %collective-permute-done.1 = f32[18,81,128]{2,1,0:T(8,128)S(1)} collective-permute-done((f32[18,81,128]{2,1,0:T(8,128)S(1)}, f32[18,81,128]{2,1,0:T(8,128)S(1)}, u32[]{:S(2)}, u32[]{:S(2)}) %collective-permute-start.1) | collective-permute-done | bytes 746528 | tf_op jit(solution)/shard_map/ppermute | solution.py:21
  113.8 1.2 collective-permute-done
  115.0 0.7 copy_add_fusion
  115.7 0.1 slice_select_fusion.2
  115.8 0.1 slice_select_fusion.3
  115.9 0.1 copy.63
  116.0 0.1 copy.64
  116.1 1.6 collective-permute-start.3
  117.7 0.5 collective-permute-start.2
  118.2 7.7 %collective-permute-done.3 = f32[9,81,128]{2,1,0:T(8,128)S(1)} collective-permute-done((f32[9,81,128]{2,1,0:T(8,128)S(1)}, f32[9,81,128]{2,1,0:T(8,128)S(1)}, u32[]{:S(2)}, u32[]{:S(2)}) %collective-permute-start.3) | collective-permute-done | bytes 373280 | tf_op jit(solution)/shard_map/ppermute | solution.py:21
  125.9 1.2 collective-permute-done.2
  127.1 0.2 copy_add_fusion.2
  127.3 0.2 copy_add_fusion.3
  127.5 0.1 copy.67
  127.6 0.1 copy.68
  127.8 0.6 collective-permute-start.5
  128.4 0.6 collective-permute-start.4
  129.0 7.4 %collective-permute-done.5 = f32[9,81,128]{2,1,0:T(8,128)S(1)} collective-permute-done((f32[9,81,128]{2,1,0:T(8,128)S(1)}, f32[9,81,128]{2,1,0:T(8,128)S(1)}, u32[]{:S(2)}, u32[]{:S(2)}) %collective-permute-start.5) | collective-permute-done | bytes 373280 | tf_op jit(solution)/shard_map/ppermute | solution.py:21
  136.4 0.3 collective-permute-done.4
  136.6 0.1 copy.82
  136.7 0.1 maximum_select_fusion.2
  136.8 0.2 copy.70
  137.1 0.1 copy.81
  137.2 0.1 maximum_select_fusion.3
  137.3 0.2 copy.72
  137.5 1.6 collective-permute-start.6
  139.1 0.6 collective-permute-start.7
  139.7 14.0 %collective-permute-done.6 = f32[18,81,128]{2,1,0:T(8,128)S(1)} collective-permute-done((f32[18,81,128]{2,1,0:T(8,128)S(1)}, f32[18,81,128]{2,1,0:T(8,128)S(1)}, u32[]{:S(2)}, u32[]{:S(2)}) %collective-permute-start.6) | collective-permute-done | bytes 746528 | tf_op jit(solution)/shard_map/ppermute | solution.py:21
  153.7 1.1 collective-permute-done.7
  154.8 0.1 maximum_select_fusion.1
  154.9 0.1 maximum_select_fusion
  155.1 0.5 fusion
  155.5 2.0 %copy.73 = f32[64,81,128]{2,0,1:T(8,128)} copy(f32[64,81,128]{2,1,0:T(8,128)S(1)} %fusion) | data formatting | bytes 5308416 | tf_op jit(solution)/shard_map/div | solution.py:17
  (9 shorter events, 0.1 us)
Async XLA Ops:
  7.2 6.5 %copy-start.1 = (s32[24]{0:T(128)S(1)}, s32[24]{0:T(128)}, u32[]{:S(2)}) copy-start(s32[24]{0:T(128)} %param.4) | copy-start | bytes 292
  7.2 6.5 %copy-start = (bf16[64,24,280]{2,1,0:T(8,128)(2,1)S(1)}, bf16[64,24,280]{2,1,0:T(8,128)(2,1)}, u32[]{:S(2)}) copy-start(bf16[64,24,280]{2,1,0:T(8,128)(2,1)} %param.3) | copy-start | bytes 2580484
  7.2 61.1 %all-to-all-start = ((bf16[128,24,280]{2,1,0:T(8,128)(2,1)}), bf16[128,24,280]{2,1,0:T(8,128)(2,1)S(1)}, u32[]{:S(2)}, u32[]{:S(2)}) async-start(bf16[128,24,280]{2,1,0:T(8,128)(2,1)} %copy.54), calls=%async_computation | async-start | bytes 4718592 | tf_op jit(solution)/shard_map/all_to_all | solution.py:95
  94.1 19.7 %collective-permute-start.1 = (f32[18,81,128]{2,1,0:T(8,128)S(1)}, f32[18,81,128]{2,1,0:T(8,128)S(1)}, u32[]{:S(2)}, u32[]{:S(2)}) collective-permute-start(f32[18,81,128]{2,1,0:T(8,128)S(1)} %copy.60), channel_id=1, source_target_pairs={{0,16},{8,24},{16,0},{24,8},{1,17},{9,25},{17,1},{25,9},{2,18},{10... | collective-permute-start | bytes 2239496 | tf_op jit(solution)/shard_map/ppermute | solution.py:21
  95.7 19.3 %collective-permute-start = (f32[18,81,128]{2,1,0:T(8,128)S(1)}, f32[18,81,128]{2,1,0:T(8,128)S(1)}, u32[]{:S(2)}, u32[]{:S(2)}) collective-permute-start(f32[18,81,128]{2,1,0:T(8,128)S(1)} %copy.59), channel_id=1, source_target_pairs={{0,8},{8,0},{16,24},{24,16},{1,9},{9,1},{17,25},{25,17},{2,10},{10... | collective-permute-start | bytes 2239496 | tf_op jit(solution)/shard_map/ppermute | solution.py:21
  116.1 9.8 %collective-permute-start.3 = (f32[9,81,128]{2,1,0:T(8,128)S(1)}, f32[9,81,128]{2,1,0:T(8,128)S(1)}, u32[]{:S(2)}, u32[]{:S(2)}) collective-permute-start(f32[9,81,128]{2,1,0:T(8,128)S(1)} %copy.64), channel_id=1, source_target_pairs={{0,8},{8,0},{16,24},{24,16},{1,9},{9,1},{17,25},{25,17},{2,10},{10... | collective-permute-start | bytes 1119752 | tf_op jit(solution)/shard_map/ppermute | solution.py:21
  117.7 9.4 %collective-permute-start.2 = (f32[9,81,128]{2,1,0:T(8,128)S(1)}, f32[9,81,128]{2,1,0:T(8,128)S(1)}, u32[]{:S(2)}, u32[]{:S(2)}) collective-permute-start(f32[9,81,128]{2,1,0:T(8,128)S(1)} %copy.63), channel_id=1, source_target_pairs={{0,16},{8,24},{16,0},{24,8},{1,17},{9,25},{17,1},{25,9},{2,18},{10... | collective-permute-start | bytes 1119752 | tf_op jit(solution)/shard_map/ppermute | solution.py:21
  127.8 8.6 %collective-permute-start.5 = (f32[9,81,128]{2,1,0:T(8,128)S(1)}, f32[9,81,128]{2,1,0:T(8,128)S(1)}, u32[]{:S(2)}, u32[]{:S(2)}) collective-permute-start(f32[9,81,128]{2,1,0:T(8,128)S(1)} %copy.68), channel_id=1, source_target_pairs={{0,8},{8,0},{16,24},{24,16},{1,9},{9,1},{17,25},{25,17},{2,10},{10... | collective-permute-start | bytes 1119752 | tf_op jit(solution)/shard_map/ppermute | solution.py:21
  128.4 8.3 %collective-permute-start.4 = (f32[9,81,128]{2,1,0:T(8,128)S(1)}, f32[9,81,128]{2,1,0:T(8,128)S(1)}, u32[]{:S(2)}, u32[]{:S(2)}) collective-permute-start(f32[9,81,128]{2,1,0:T(8,128)S(1)} %copy.67), channel_id=1, source_target_pairs={{0,16},{8,24},{16,0},{24,8},{1,17},{9,25},{17,1},{25,9},{2,18},{10... | collective-permute-start | bytes 1119752 | tf_op jit(solution)/shard_map/ppermute | solution.py:21
  137.5 16.2 %collective-permute-start.6 = (f32[18,81,128]{2,1,0:T(8,128)S(1)}, f32[18,81,128]{2,1,0:T(8,128)S(1)}, u32[]{:S(2)}, u32[]{:S(2)}) collective-permute-start(f32[18,81,128]{2,1,0:T(8,128)S(1)} %bitcast.31), channel_id=1, source_target_pairs={{0,8},{8,0},{16,24},{24,16},{1,9},{9,1},{17,25},{25,17},{2,10},{10... | collective-permute-start | bytes 2239496 | tf_op jit(solution)/shard_map/ppermute | solution.py:21
  139.1 15.7 %collective-permute-start.7 = (f32[18,81,128]{2,1,0:T(8,128)S(1)}, f32[18,81,128]{2,1,0:T(8,128)S(1)}, u32[]{:S(2)}, u32[]{:S(2)}) collective-permute-start(f32[18,81,128]{2,1,0:T(8,128)S(1)} %bitcast.33), channel_id=1, source_target_pairs={{0,16},{8,24},{16,0},{24,8},{1,17},{9,25},{17,1},{25,9},{2,18},{10... | collective-permute-start | bytes 2239496 | tf_op jit(solution)/shard_map/ppermute | solution.py:21

commit v4 on v2

--- a/solution.py
+++ b/solution.py
@@ -44,15 +44,12 @@
     return acc
 
 
-def sta_allreduce(data):
+def sta_allreduce(data, order):
     size = lax.axis_size("sta")
     if size & (size - 1) or size == 1:
         return lax.psum(data, "sta")
     bits = [1 << k for k in range(size.bit_length() - 1)]
-    half = data.shape[0] // 2
-    first = halving_allreduce(data[:half], "sta", bits)
-    second = halving_allreduce(data[half:], "sta", bits[::-1])
-    return jnp.concatenate([first, second], axis=0)
+    return halving_allreduce(data, "sta", bits[::-1] if order else bits)
 
 
 def body(traces, channel_valid, partner_block):
@@ -92,14 +89,6 @@
     )
     valid = channel_valid.astype(jnp.bfloat16)
     template = traces[:, :, MAXLAG : MAXLAG + WIN] * valid[None, :, None]
-    lag_scores = lax.conv_general_dilated(
-        received,
-        template,
-        (1,),
-        "VALID",
-        dimension_numbers=("NCH", "OIH", "CHN"),
-        preferred_element_type=jnp.float32,
-    )
     event_energy = jnp.sum(jnp.square(template.astype(jnp.float32)), axis=(1, 2))
     squares_sum = jnp.sum(
         jnp.square(received.astype(jnp.float32)) * channel_valid.astype(jnp.float32)[None, :, None],
@@ -111,14 +100,31 @@
         (((0,), (1,)), ((), ())),
         precision=lax.Precision.HIGHEST,
     )
-    extra = 2 * sta_size
     pad = jnp.zeros((lag_count * slot_count - events,), jnp.float32)
     energy_row = jnp.concatenate([event_energy, pad]).reshape(1, lag_count, slot_count)
-    filler = jnp.zeros((extra - 2, lag_count, slot_count), jnp.float32)
-    packed = jnp.concatenate([lag_scores, slot_energy[None], energy_row, filler], axis=0)
-    total = sta_allreduce(packed)
-    event_all = total[events + 1].reshape(-1)[:events]
-    return normalize(total[:events], total[events], event_all)
+    split = events // 2
+    totals = []
+    for h, (low, high) in enumerate([(0, split), (split, events)]):
+        lag_scores = lax.conv_general_dilated(
+            received,
+            template[low:high],
+            (1,),
+            "VALID",
+            dimension_numbers=("NCH", "OIH", "CHN"),
+            preferred_element_type=jnp.float32,
+        )
+        rows = [lag_scores]
+        if h == 0:
+            rows += [slot_energy[None], energy_row]
+        count = sum(r.shape[0] for r in rows)
+        spare = -count % sta_size
+        if spare:
+            rows.append(jnp.zeros((spare, lag_count, slot_count), jnp.float32))
+        totals.append(sta_allreduce(jnp.concatenate(rows, axis=0), h))
+    first, second = totals
+    scores_all = jnp.concatenate([first[:split], second[: events - split]], axis=0)
+    event_all = first[split + 1].reshape(-1)[:events]
+    return normalize(scores_all, first[split], event_all)
 
 
 def solution(mesh):

time: 183 us -> 170 us (0.929)
  waiting for transfers between devices: 124 us -> 91.7 us
  matrix products: 18.4 us -> 33.9 us
    ppermute x8, waiting for transfers between devices: 74.6 us -> 44.3 us  [exchange(): return lax.ppermute(value, axis, [(i, i ^ bit) for i in range(size)])]
    conv_general_dilated x1 -> x2, matrix products: 17.2 us -> 32.6 us  [body(): lax.conv_general_dilated(received, template[low:high], (1,), 'VALID', dim...]
    mul x1 -> x0, local copies, waits for them, and re-layouts: 2.88 us -> none  [body(): template = traces[:, :, MAXLAG:MAXLAG + WIN] * valid[None, :, None]]
    unnamed x5 -> x16, local copies, waits for them, and re-layouts: 0.77 us -> 3.65 us
    all_to_all x1, waiting for transfers between devices: 49.8 us -> 47.5 us  [body(): lax.all_to_all(outgoing.reshape(slot_count, channels, extent), 'evt', spl...]
    ppermute x8, starting transfers between devices: 8.83 us -> 10.7 us  [exchange(): return lax.ppermute(value, axis, [(i, i ^ bit) for i in range(size)])]
  transfers between devices with their start and end apart: 9 -> 9, of which waited for: 8 -> 9; matrix products, arithmetic and copies ran while one was open for 3% -> 9% of each run, Pallas kernels for 0% -> 0%
where the time goes in v4:
time: 170 us
  waiting for transfers between devices  91.7 us (54%)
  matrix products  33.9 us (20%)
  local copies, waits for them, and re-layouts  18.7 us (11%)
  starting transfers between devices  17.1 us (10%)
  other arithmetic  8.42 us (5%)
    all_to_all x1, waiting for transfers between devices, body(): lax.all_to_all(outgoing.reshape(slot_count, channels, extent), 'evt', spl...  47.5 us
    ppermute x8, waiting for transfers between devices, exchange(): return lax.ppermute(value, axis, [(i, i ^ bit) for i in range(size)])  44.3 us
    conv_general_dilated x2, matrix products, body(): lax.conv_general_dilated(received, template[low:high], (1,), 'VALID', dim...  32.6 us
    ppermute x8, starting transfers between devices, exchange(): return lax.ppermute(value, axis, [(i, i ^ bit) for i in range(size)])  10.7 us
    all_to_all x1, starting transfers between devices, body(): lax.all_to_all(outgoing.reshape(slot_count, channels, extent), 'evt', spl...  6.46 us
    all_to_all x2, local copies, waits for them, and re-layouts, body(): lax.all_to_all(outgoing.reshape(slot_count, channels, extent), 'evt', spl...  5.43 us
    unnamed x16, local copies, waits for them, and re-layouts  3.65 us
  transfers between devices with their start and end apart: 9, of which 9 were waited for; matrix products, arithmetic and copies ran while one was open for 9% of the time, Pallas kernels for 0%

profile of v4, /device:TPU:0, one launch (start us, length us, event | category | flops | bytes accessed | tf_op | source)
XLA Modules:
  0.0 170.1 jit_solution(1318211979880062174)
XLA Ops:
  0.0 0.8 copy.52
  0.8 0.1 reshape.120
  0.9 0.1 fusion.9
  1.0 0.2 reduce_window_sum.11
  1.2 0.2 select_reduce_fusion
  1.4 2.1 %reshape.121 = bf16[64,6720]{1,0:T(8,128)(2,1)S(1)} reshape(bf16[64,24,280]{2,1,0:T(8,128)(2,1)} %param.3) | data formatting | bytes 1720320 | tf_op jit(solution)/shard_map/reshape | solution.py:81
  3.5 0.9 convolution_convert_fusion
  4.4 2.7 %copy.53 = bf16[128,24,280]{2,1,0:T(8,128)(2,1)} copy(bf16[128,24,280]{0,2,1:T(8,128)(2,1)S(1)} %bitcast.25) | data formatting | bytes 3440640 | tf_op jit(solution)/shard_map/reshape | solution.py:84
  7.2 6.5 %all-to-all-start = ((bf16[128,24,280]{2,1,0:T(8,128)(2,1)}), bf16[128,24,280]{2,1,0:T(8,128)(2,1)S(1)}, u32[]{:S(2)}, u32[]{:S(2)}) async-start(bf16[128,24,280]{2,1,0:T(8,128)(2,1)} %copy.53), calls=%async_computation | async-start | bytes 4718592 | tf_op jit(solution)/shard_map/all_to_all | solution.py:83
  13.6 0.0 copy-done.3
  13.6 0.0 copy-start.6
  13.6 1.2 slice.62
  14.9 2.9 %copy.72 = bf16[64,24,200]{0,1,2:T(8,128)(2,1)} copy(bf16[64,24,200]{2,1,0:T(8,128)(2,1)} %slice.62) | data formatting | bytes 1228800
  17.7 0.0 copy-done.6
  17.7 2.9 %multiply_reduce_fusion.1 = (f32[64]{0:T(128)S(1)}, bf16[64,24,200]{0,1,2:T(8,128)(2,1)}) fusion(bf16[64,24,200]{0,1,2:T(8,128)(2,1)} %copy.72, bf16[24]{0:T(256)(128)(2,1)S(1)} %get-tuple-element.12), kind=kLoop, calls=%fused_computation.3 | loop fusion | flops 1228736 | bytes 1229104 | tf_op jit(solution)/shard_map/reduce_sum | solution.py:92
  20.8 0.1 pad_slice_fusion
  20.8 47.5 %all-to-all-done = bf16[128,24,280]{2,1,0:T(8,128)(2,1)S(1)} async-done(((bf16[128,24,280]{2,1,0:T(8,128)(2,1)}), bf16[128,24,280]{2,1,0:T(8,128)(2,1)S(1)}, u32[]{:S(2)}, u32[]{:S(2)}) %all-to-all-start) | async-done | bytes 1720352 | tf_op jit(solution)/shard_map/all_to_all | solution.py:83
  68.3 2.8 %copy.55 = bf16[128,24,280]{0,1,2:T(8,128)(2,1)} copy(bf16[128,24,280]{2,1,0:T(8,128)(2,1)S(1)} %all-to-all-done) | data formatting | bytes 3440640 | tf_op jit(solution)/shard_map/all_to_all | solution.py:83
  71.2 16.7 %fusion = f32[32,81,128]{2,0,1:T(8,128)S(1)} fusion(bf16[128,24,280]{0,1,2:T(8,128)(2,1)} %copy.55, bf16[64,24,200]{0,1,2:T(8,128)(2,1)} %get-tuple-element.6), kind=kOutput, calls=%fused_computation.7 | convolution fusion | flops 3185049600 | bytes 3661824 | tf_op jit(solution)/shard_map/conv_general_dilated | solution.py:108
  87.8 0.0 copy-done.4
  87.8 0.0 copy-done.5
  87.9 0.0 copy-start.1
  87.9 15.9 %fusion.2 = f32[32,81,128]{2,0,1:T(8,128)} fusion(bf16[128,24,280]{0,1,2:T(8,128)(2,1)S(1)} %copy-done.4, bf16[64,24,200]{0,1,2:T(8,128)(2,1)S(1)} %copy-done.5), kind=kOutput, calls=%fused_computation.9 | convolution fusion | flops 3185049600 | bytes 3661824 | tf_op jit(solution)/shard_map/conv_general_dilated | solution.py:108
  103.8 0.0 copy-done.1
  103.8 0.9 slice_select_fusion.1
  104.7 1.5 collective-permute-start.4
  106.2 2.6 %copy.56 = bf16[128,24,280]{0,2,1:T(8,128)(2,1)} copy(bf16[128,24,280]{2,1,0:T(8,128)(2,1)S(1)} %all-to-all-done) | data formatting | bytes 3440640 | tf_op jit(solution)/shard_map/all_to_all | solution.py:83
  108.8 2.0 %multiply_reduce_fusion = f32[128,280]{0,1:T(8,128)S(1)} fusion(bf16[128,24,280]{0,2,1:T(8,128)(2,1)} %copy.56, f32[24]{0:T(128)S(1)} %get-tuple-element.11), kind=kLoop, calls=%fused_computation.1 | loop fusion | flops 3404800 | bytes 1863776 | tf_op jit(solution)/shard_map/reduce_sum | solution.py:93
  110.9 0.3 fusion.6
  111.3 0.3 slice_select_fusion
  111.6 0.2 copy.58
  111.8 1.6 collective-permute-start
  113.3 8.1 %collective-permute-done.4 = f32[16,81,128]{2,0,1:T(8,128)S(1)} collective-permute-done((f32[16,81,128]{2,0,1:T(8,128)}, f32[16,81,128]{2,0,1:T(8,128)S(1)}, u32[]{:S(2)}, u32[]{:S(2)}) %collective-permute-start.4) | collective-permute-done | bytes 663584 | tf_op jit(solution)/shard_map/ppermute | solution.py:21
  121.4 0.0 copy-done.2
  121.4 0.1 select_add_fusion
  121.6 1.6 collective-permute-start.5
  123.1 9.7 %collective-permute-done = f32[18,81,128]{2,1,0:T(8,128)S(1)} collective-permute-done((f32[18,81,128]{2,1,0:T(8,128)S(1)}, f32[18,81,128]{2,1,0:T(8,128)S(1)}, u32[]{:S(2)}, u32[]{:S(2)}) %collective-permute-start) | collective-permute-done | bytes 746528 | tf_op jit(solution)/shard_map/ppermute | solution.py:21
  132.8 0.4 copy_add_fusion
  133.3 0.1 slice_select_fusion.2
  133.4 0.1 copy.60
  133.5 0.6 collective-permute-start.1
  134.1 4.2 %collective-permute-done.5 = f32[8,81,128]{2,0,1:T(8,128)S(1)} collective-permute-done((f32[8,81,128]{2,0,1:T(8,128)S(1)}, f32[8,81,128]{2,0,1:T(8,128)S(1)}, u32[]{:S(2)}, u32[]{:S(2)}) %collective-permute-start.5) | collective-permute-done | bytes 331808 | tf_op jit(solution)/shard_map/ppermute | solution.py:21
  138.3 0.1 select_add_fusion.1
  138.3 1.6 collective-permute-start.6
  139.9 2.2 %collective-permute-done.1 = f32[9,81,128]{2,1,0:T(8,128)S(1)} collective-permute-done((f32[9,81,128]{2,1,0:T(8,128)S(1)}, f32[9,81,128]{2,1,0:T(8,128)S(1)}, u32[]{:S(2)}, u32[]{:S(2)}) %collective-permute-start.1) | collective-permute-done | bytes 373280 | tf_op jit(solution)/shard_map/ppermute | solution.py:21
  142.1 0.2 copy_add_fusion.1
  142.3 0.1 copy.62
  142.4 0.6 collective-permute-start.2
  143.0 3.6 %collective-permute-done.6 = f32[8,81,128]{2,0,1:T(8,128)S(1)} collective-permute-done((f32[8,81,128]{2,0,1:T(8,128)S(1)}, f32[8,81,128]{2,0,1:T(8,128)S(1)}, u32[]{:S(2)}, u32[]{:S(2)}) %collective-permute-start.6) | collective-permute-done | bytes 331808 | tf_op jit(solution)/shard_map/ppermute | solution.py:21
  146.5 0.1 copy_bitcast_fusion.2
  146.6 0.6 collective-permute-start.7
  147.2 6.8 %collective-permute-done.2 = f32[9,81,128]{2,1,0:T(8,128)S(1)} collective-permute-done((f32[9,81,128]{2,1,0:T(8,128)S(1)}, f32[9,81,128]{2,1,0:T(8,128)S(1)}, u32[]{:S(2)}, u32[]{:S(2)}) %collective-permute-start.2) | collective-permute-done | bytes 373280 | tf_op jit(solution)/shard_map/ppermute | solution.py:21
  154.0 0.1 copy.78
  154.1 0.1 maximum_select_fusion.1
  154.2 0.2 copy.64
  154.4 2.8 %collective-permute-start.3 = (f32[18,81,128]{2,1,0:T(8,128)S(1)}, f32[18,81,128]{2,1,0:T(8,128)S(1)}, u32[]{:S(2)}, u32[]{:S(2)}) collective-permute-start(f32[18,81,128]{2,1,0:T(8,128)S(1)} %bitcast.30), channel_id=1, source_target_pairs={{0,8},{8,0},{16,24},{24,16},{1,9},{9,1},{17,25},{25,17},{2,10},{10... | collective-permute-start | bytes 2239496 | tf_op jit(solution)/shard_map/ppermute | solution.py:21
  157.2 7.4 %collective-permute-done.7 = f32[16,81,128]{2,0,1:T(8,128)S(1)} collective-permute-done((f32[16,81,128]{2,0,1:T(8,128)S(1)}, f32[16,81,128]{2,0,1:T(8,128)S(1)}, u32[]{:S(2)}, u32[]{:S(2)}) %collective-permute-start.7) | collective-permute-done | bytes 663584 | tf_op jit(solution)/shard_map/ppermute | solution.py:21
  164.6 0.1 maximum_select_fusion.2
  164.7 0.4 copy.69
  165.1 2.3 %collective-permute-done.3 = f32[18,81,128]{2,1,0:T(8,128)S(1)} collective-permute-done((f32[18,81,128]{2,1,0:T(8,128)S(1)}, f32[18,81,128]{2,1,0:T(8,128)S(1)}, u32[]{:S(2)}, u32[]{:S(2)}) %collective-permute-start.3) | collective-permute-done | bytes 746528 | tf_op jit(solution)/shard_map/ppermute | solution.py:21
  167.4 0.1 maximum_select_fusion
  167.6 0.1 slice.82
  167.7 0.5 maximum_multiply_fusion
  168.1 2.0 %copy.70 = f32[64,81,128]{2,0,1:T(8,128)} copy(f32[64,81,128]{2,1,0:T(8,128)S(1)} %maximum_multiply_fusion) | data formatting | bytes 5308416 | tf_op jit(solution)/shard_map/div | solution.py:17
  (16 shorter events, 0.2 us)
Async XLA Ops:
  7.2 6.5 %copy-start.3 = (bf16[64,24,280]{2,1,0:T(8,128)(2,1)S(1)}, bf16[64,24,280]{2,1,0:T(8,128)(2,1)}, u32[]{:S(2)}) copy-start(bf16[64,24,280]{2,1,0:T(8,128)(2,1)} %param.3) | copy-start | bytes 2580484
  7.2 61.1 %all-to-all-start = ((bf16[128,24,280]{2,1,0:T(8,128)(2,1)}), bf16[128,24,280]{2,1,0:T(8,128)(2,1)S(1)}, u32[]{:S(2)}, u32[]{:S(2)}) async-start(bf16[128,24,280]{2,1,0:T(8,128)(2,1)} %copy.53), calls=%async_computation | async-start | bytes 4718592 | tf_op jit(solution)/shard_map/all_to_all | solution.py:83
  13.6 4.1 %copy-start.6 = (s32[24]{0:T(128)S(1)}, s32[24]{0:T(128)}, u32[]{:S(2)}) copy-start(s32[24]{0:T(128)} %param.4) | copy-start | bytes 292
  71.1 16.7 %copy-start.4 = (bf16[128,24,280]{0,1,2:T(8,128)(2,1)S(1)}, bf16[128,24,280]{0,1,2:T(8,128)(2,1)}, u32[]{:S(2)}) copy-start(bf16[128,24,280]{0,1,2:T(8,128)(2,1)} %copy.55) | copy-start | bytes 5160964
  71.2 16.7 %copy-start.5 = (bf16[64,24,200]{0,1,2:T(8,128)(2,1)S(1)}, bf16[64,24,200]{0,1,2:T(8,128)(2,1)}, u32[]{:S(2)}) copy-start(bf16[64,24,200]{0,1,2:T(8,128)(2,1)} %get-tuple-element.6) | copy-start | bytes 1843204
  87.9 16.0 %copy-start.1 = (f32[32,81,128]{2,0,1:T(8,128)}, f32[32,81,128]{2,0,1:T(8,128)S(1)}, u32[]{:S(2)}) copy-start(f32[32,81,128]{2,0,1:T(8,128)S(1)} %fusion) | copy-start | bytes 3981316
  104.7 16.7 %collective-permute-start.4 = (f32[16,81,128]{2,0,1:T(8,128)}, f32[16,81,128]{2,0,1:T(8,128)S(1)}, u32[]{:S(2)}, u32[]{:S(2)}) collective-permute-start(f32[16,81,128]{2,0,1:T(8,128)} %slice_select_fusion.1), channel_id=1, source_target_pairs={{0,16},{8,24},{16,0},{24,8},{1,17},{9,25},{17,1},{25,9},{2,18},{10... | collective-permute-start | bytes 1990664 | tf_op jit(solution)/shard_map/ppermute | solution.py:21
  108.8 2.4 %copy-start = (f32[32,81,128]{2,0,1:T(8,128)S(1)}, f32[32,81,128]{2,0,1:T(8,128)}, u32[]{:S(2)}) copy-start(f32[32,81,128]{2,0,1:T(8,128)} %fusion.2) | copy-start | bytes 3981316
  111.6 9.8 %copy-start.2 = (f32[32,81,128]{2,0,1:T(8,128)S(1)}, f32[32,81,128]{2,0,1:T(8,128)}, u32[]{:S(2)}) copy-start(f32[32,81,128]{2,0,1:T(8,128)} %copy-done.1) | copy-start | bytes 3981316
  111.8 21.1 %collective-permute-start = (f32[18,81,128]{2,1,0:T(8,128)S(1)}, f32[18,81,128]{2,1,0:T(8,128)S(1)}, u32[]{:S(2)}, u32[]{:S(2)}) collective-permute-start(f32[18,81,128]{2,1,0:T(8,128)S(1)} %copy.58), channel_id=1, source_target_pairs={{0,8},{8,0},{16,24},{24,16},{1,9},{9,1},{17,25},{25,17},{2,10},{10... | collective-permute-start | bytes 2239496 | tf_op jit(solution)/shard_map/ppermute | solution.py:21
  121.6 16.7 %collective-permute-start.5 = (f32[8,81,128]{2,0,1:T(8,128)S(1)}, f32[8,81,128]{2,0,1:T(8,128)S(1)}, u32[]{:S(2)}, u32[]{:S(2)}) collective-permute-start(f32[8,81,128]{2,0,1:T(8,128)S(1)} %slice_select_fusion.3), channel_id=1, source_target_pairs={{0,8},{8,0},{16,24},{24,16},{1,9},{9,1},{17,25},{25,17},{2,10},{10... | collective-permute-start | bytes 995336 | tf_op jit(solution)/shard_map/ppermute | solution.py:21
  133.5 8.6 %collective-permute-start.1 = (f32[9,81,128]{2,1,0:T(8,128)S(1)}, f32[9,81,128]{2,1,0:T(8,128)S(1)}, u32[]{:S(2)}, u32[]{:S(2)}) collective-permute-start(f32[9,81,128]{2,1,0:T(8,128)S(1)} %copy.60), channel_id=1, source_target_pairs={{0,16},{8,24},{16,0},{24,8},{1,17},{9,25},{17,1},{25,9},{2,18},{10... | collective-permute-start | bytes 1119752 | tf_op jit(solution)/shard_map/ppermute | solution.py:21
  138.3 8.2 %collective-permute-start.6 = (f32[8,81,128]{2,0,1:T(8,128)S(1)}, f32[8,81,128]{2,0,1:T(8,128)S(1)}, u32[]{:S(2)}, u32[]{:S(2)}) collective-permute-start(f32[8,81,128]{2,0,1:T(8,128)S(1)} %select_add_fusion.1), channel_id=1, source_target_pairs={{0,8},{8,0},{16,24},{24,16},{1,9},{9,1},{17,25},{25,17},{2,10},{10... | collective-permute-start | bytes 995336 | tf_op jit(solution)/shard_map/ppermute | solution.py:21
  142.4 11.6 %collective-permute-start.2 = (f32[9,81,128]{2,1,0:T(8,128)S(1)}, f32[9,81,128]{2,1,0:T(8,128)S(1)}, u32[]{:S(2)}, u32[]{:S(2)}) collective-permute-start(f32[9,81,128]{2,1,0:T(8,128)S(1)} %copy.62), channel_id=1, source_target_pairs={{0,16},{8,24},{16,0},{24,8},{1,17},{9,25},{17,1},{25,9},{2,18},{10... | collective-permute-start | bytes 1119752 | tf_op jit(solution)/shard_map/ppermute | solution.py:21
  146.6 18.0 %collective-permute-start.7 = (f32[16,81,128]{2,0,1:T(8,128)S(1)}, f32[16,81,128]{2,0,1:T(8,128)S(1)}, u32[]{:S(2)}, u32[]{:S(2)}) collective-permute-start(f32[16,81,128]{2,0,1:T(8,128)S(1)} %get-tuple-element.9), channel_id=1, source_target_pairs={{0,16},{8,24},{16,0},{24,8},{1,17},{9,25},{17,1},{25,9},{2,18},{10... | collective-permute-start | bytes 1990664 | tf_op jit(solution)/shard_map/ppermute | solution.py:21
  154.4 13.0 %collective-permute-start.3 = (f32[18,81,128]{2,1,0:T(8,128)S(1)}, f32[18,81,128]{2,1,0:T(8,128)S(1)}, u32[]{:S(2)}, u32[]{:S(2)}) collective-permute-start(f32[18,81,128]{2,1,0:T(8,128)S(1)} %bitcast.30), channel_id=1, source_target_pairs={{0,8},{8,0},{16,24},{24,16},{1,9},{9,1},{17,25},{25,17},{2,10},{10... | collective-permute-start | bytes 2239496 | tf_op jit(solution)/shard_map/ppermute | solution.py:21
